TPU v7x, 32 devices: a whole 2x2x4 slice. The times are simulated.
32 devices in a mesh: row: 4 (over y, x), col: 8 (over z, core).
Axes of the slice: x: 2, y: 2, z: 4, core: 2. Of those that a mesh axis runs over, the one named last changes fastest.
Arguments:
- tokens: bfloat16 [256, 12288], P('col', 'row'), may hold values from -6 to 6
- weight: bfloat16 [12288, 24576], P('row', 'col'), may hold values from -0.0546875 to 0.0546875
- bias: float32 [24576], P('col'), may hold values from -4 to 4
- cotangent: bfloat16 [256, 24576], P(None, 'col'), may hold values from -6 to 6
Outputs:
- hidden: bfloat16 [256, 24576], P('row', 'col')
- grad_tokens: bfloat16 [256, 12288], P('col', 'row')
- grad_weight: bfloat16 [12288, 24576], P('row', 'col')
- grad_bias: float32 [24576], P('col')
All inputs are finite; a program needn't handle non-finite values.
Results may differ from a plain program's by a relative error of at most 0.0055.
Values may be sent and summed in bfloat16 or wider, within the bound.
No kernel may reach another device: no remote copies, remote signals or barrier semaphores. Data moves between devices by JAX's collectives and lax.ppermute only.
A program may use at most 192 MiB of HBM per device.

v0:
```python
import math
import jax
import jax.numpy as jnp
from jax import lax
from jax.sharding import PartitionSpec as P


def activate(preact, cotangent):
    normal_cdf = 0.5 * (1.0 + jax.scipy.special.erf(preact / math.sqrt(2.0)))
    normal_pdf = jnp.exp(-0.5 * preact * preact) / math.sqrt(2.0 * math.pi)
    hidden = (preact * normal_cdf).astype(jnp.bfloat16)
    grad_pre = (cotangent.astype(jnp.float32) * (normal_cdf + preact * normal_pdf)).astype(
        jnp.bfloat16
    )
    return (hidden, grad_pre)


def body(tokens, weight, bias, cotangent):
    local_x = lax.all_gather(tokens, "col", axis=0, tiled=True)
    total_rows = local_x.shape[0]
    my_rows = total_rows // lax.axis_size("row")
    first_row = lax.axis_index("row") * my_rows
    partial_value = jnp.dot(local_x, weight, preferred_element_type=jnp.float32)
    preact = lax.psum(partial_value, "row") + bias
    all_hidden, full_grad = activate(preact, cotangent)
    hidden = lax.dynamic_slice_in_dim(all_hidden, first_row, my_rows, 0)
    grad_tokens = lax.psum_scatter(
        lax.dot_general(
            full_grad, weight, (((1,), (1,)), ((), ())), preferred_element_type=jnp.float32
        ),
        "col",
        scatter_dimension=0,
        tiled=True,
    ).astype(jnp.bfloat16)
    grad_weight = lax.dot_general(
        local_x, full_grad, (((0,), (0,)), ((), ())), preferred_element_type=jnp.float32
    ).astype(jnp.bfloat16)
    grad_bias = jnp.sum(full_grad.astype(jnp.float32), axis=0)
    return (hidden, grad_tokens, grad_weight, grad_bias)


def solution(mesh):
    placed = (P("col", "row"), P("row", "col"), P("col"), P(None, "col"))
    return jax.shard_map(
        body,
        mesh=mesh,
        in_specs=placed,
        out_specs=(P("row", "col"), P("col", "row"), P("row", "col"), P("col")),
        check_vma=False,
    )
```

profile of v0, /device:TPU:0, one launch (start us, length us, event | category | flops | bytes accessed | tf_op | source)
XLA Modules:
  0.0 199.8 jit_solution(12277951146830679832)
XLA Ops:
  7.2 0.0 all-gather.2.cloned.1.call-start
  7.2 0.7 all-gather.2.cloned.1.call-update
  7.9 0.0 all-reduce.2.cloned.1.call-start
  7.9 29.5 %all-gather.2.cloned.1.call-done = bf16[256,3072]{1,0:T(8,128)(2,1)} async-done(((bf16[32,3072]{1,0:T(8,128)(2,1)}), bf16[256,3072]{1,0:T(8,128)(2,1)}) %all-gather.2.cloned.1.call-update) | async-done | bytes 1572880 | tf_op jit(solution)/shard_map/all_gather | solution.py:19
  37.4 10.6 %fusion.8 = f32[256,3072]{1,0:T(8,128)} fusion(bf16[256,3072]{1,0:T(8,128)(2,1)} %all-gather.2.cloned.1.call-done, bf16[3072,3072]{1,0:T(8,128)(2,1)} %param.5), kind=kOutput, calls=%fused_computation.13 | convolution fusion | flops 4831838208 | bytes 23592960 | tf_op jit(solution)/shard_map/dot_general | solution.py:23
  48.0 0.0 copy-start.1
  48.0 0.0 copy-start.2
  48.0 0.0 all-reduce.2.cloned.1.call-update
  48.0 0.0 reduce-scatter.2.cloned.1.call-start
  48.1 86.8 %all-reduce.2.cloned.1.call-done = f32[256,3072]{1,0:T(8,128)} async-done(((f32[256,3072]{1,0:T(8,128)}), f32[256,3072]{1,0:T(8,128)}) %all-reduce.2.cloned.1.call-update) | async-done | bytes 3145744 | tf_op jit(solution)/shard_map/psum | solution.py:24
  134.9 0.0 copy-done.1
  134.9 0.0 copy-done.2
  134.9 5.4 %convert_reduce_fusion = (f32[3072]{0:T(1024)}, bf16[256,3072]{1,0:T(8,128)(2,1)S(1)}, f32[256,3072]{1,0:T(8,128)}, f32[256,3072]{1,0:T(8,128)}) fusion(bf16[256,3072]{1,0:T(8,128)(2,1)S(1)} %copy-done.1, f32[256,3072]{1,0:T(8,128)} %all-reduce.2.cloned.1.call-done, f32[3072]{0:T(1024)S(1)} %copy-done.2), kind=kLoop, calls=%fused_computation.8 | loop fusion | flops 11006976 | bytes 12607488 | tf_op jit(solution)/shard_map/reduce_sum | solution.py:38
  140.3 10.7 %fusion.9 = f32[256,3072]{1,0:T(8,128)} fusion(bf16[256,3072]{1,0:T(8,128)(2,1)S(1)} %get-tuple-element.9, bf16[3072,3072]{1,0:T(8,128)(2,1)} %param.5), kind=kOutput, calls=%fused_computation.14 | convolution fusion | flops 4831838208 | bytes 23592960 | tf_op jit(solution)/shard_map/dot_general | solution.py:28
  151.1 0.0 copy-start
  151.1 0.0 reduce-scatter.2.cloned.1.call-update
  151.1 1.4 copy-done
  152.5 9.2 %convert_bitcast_fusion = bf16[3072,3072]{0,1:T(8,128)(2,1)} fusion(bf16[256,3072]{1,0:T(8,128)(2,1)S(1)} %get-tuple-element.9, bf16[256,3072]{1,0:T(8,128)(2,1)S(1)} %copy-done), kind=kOutput, calls=%fused_computation | convolution fusion | flops 4841275392 | bytes 22020096 | tf_op jit(solution)/shard_map/dot_general | solution.py:35
  161.6 24.7 %copy.8 = bf16[3072,3072]{1,0:T(8,128)(2,1)} copy(bf16[3072,3072]{0,1:T(8,128)(2,1)} %convert_bitcast_fusion) | data formatting | bytes 37748736
  186.3 2.2 %fusion.6 = bf16[64,3072]{1,0:T(8,128)(2,1)} fusion(f32[256,3072]{1,0:T(8,128)} %get-tuple-element.10, s32[]{:T(128)S(6)} %select_n.3, f32[256,3072]{1,0:T(8,128)} %get-tuple-element.11), kind=kLoop, calls=%fused_computation.12 | loop fusion | flops 393216 | bytes 1966084 | tf_op jit(solution)/shard_map/convert_element_type | solution.py:11
  188.5 3.1 %reduce-scatter.2.cloned.1.call-done = f32[32,3072]{1,0:T(8,128)} async-done(((f32[256,3072]{1,0:T(8,128)}), f32[32,3072]{1,0:T(8,128)}) %reduce-scatter.2.cloned.1.call-update) | async-done | bytes 393232 | tf_op jit(solution)/shard_map/reduce_scatter | solution.py:27
  191.6 1.7 convert_element_type.24
Async XLA Ops:
  7.2 30.3 %all-gather.2.cloned.1.call-start = ((), (), s32[]{:S(2)}) async-start(), calls=%async_computation.1 | async-start | bytes 1769472 | tf_op jit(solution)/shard_map/all_gather | solution.py:19
  7.9 127.0 %all-reduce.2.cloned.1.call-start = ((), (), s32[]{:S(2)}) async-start(), calls=%async_computation.2 | async-start | bytes 6291456 | tf_op jit(solution)/shard_map/psum | solution.py:24
  48.0 86.9 %copy-start.1 = (bf16[256,3072]{1,0:T(8,128)(2,1)S(1)}, bf16[256,3072]{1,0:T(8,128)(2,1)}, u32[]{:S(2)}) copy-start(bf16[256,3072]{1,0:T(8,128)(2,1)} %param.7) | copy-start | bytes 4718596
  48.0 86.9 %copy-start.2 = (f32[3072]{0:T(1024)S(1)}, f32[3072]{0:T(1024)}, u32[]{:S(2)}) copy-start(f32[3072]{0:T(1024)} %param.6) | copy-start | bytes 36868
  48.0 143.6 %reduce-scatter.2.cloned.1.call-start = ((), (), s32[]{:S(2)}) async-start(), calls=%async_computation.3 | async-start | bytes 3538944 | tf_op jit(solution)/shard_map/reduce_scatter | solution.py:27
  151.1 1.4 copy-start
Sparse Core Ops, SparseCore 0:
  9.6 27.7 all-gather.1
  48.1 86.7 all-reduce.1
  151.2 40.3 reduce-scatter.1
where the time goes:
time: 201 us; the launch traced here: 200 us
  waiting for transfers between devices  120 us (60%)
  matrix products  30.4 us (15%)
  local copies, waits for them, and re-layouts  26 us (13%)
  between operations  13.8 us (7%)
  other arithmetic  9.32 us (5%)
    psum x1, waiting for transfers between devices, body(): preact = lax.psum(partial_value, 'row') + bias  86.8 us
    all_gather x1, waiting for transfers between devices, body(): local_x = lax.all_gather(tokens, 'col', axis=0, tiled=True)  29.5 us
    unnamed x7, local copies, waits for them, and re-layouts  26 us
    dot_general x1, matrix products, body(): lax.dot_general(full_grad, weight, (((1,), (1,)), ((), ())), preferred_el...  10.7 us
    dot_general x1, matrix products, body(): partial_value = jnp.dot(local_x, weight, preferred_element_type=jnp.float32)  10.6 us
    dot_general x1, matrix products, body(): lax.dot_general(local_x, full_grad, (((0,), (0,)), ((), ())), preferred_e...  9.17 us
    reduce_sum x1, other arithmetic, body(): grad_bias = jnp.sum(full_grad.astype(jnp.float32), axis=0)  5.43 us
  transfers between devices with their start and end apart: 3, of which 3 were waited for; matrix products, arithmetic and copies ran while one was open for 18% of the time, Pallas kernels for 0%

commit v1 on v0

--- a/solution.py
+++ b/solution.py
@@ -16,7 +16,12 @@
 
 
 def body(tokens, weight, bias, cotangent):
-    local_x = lax.all_gather(tokens, "col", axis=0, tiled=True)
+    ring = [tokens]
+    for hop in range(7):
+        ring.append(lax.ppermute(ring[-1], "col", [(dev, (dev + 1) % 8) for dev in range(8)]))
+    local_x = jnp.roll(
+        jnp.concatenate(ring[::-1], axis=0), (lax.axis_index("col") + 1) * ring[0].shape[0], axis=0
+    )
     total_rows = local_x.shape[0]
     my_rows = total_rows // lax.axis_size("row")
     first_row = lax.axis_index("row") * my_rows

time: 201 us -> 222 us (1.10)
  waiting for transfers between devices: 120 us -> 162 us
  local copies, waits for them, and re-layouts: 26 us -> 2.81 us
    ppermute x0 -> x7, waiting for transfers between devices: none -> 48.9 us  [body(): lax.ppermute(ring[-1], 'col', [(dev, (dev + 1) % 8) for dev in range(8)])]
    all_gather x1 -> x0, waiting for transfers between devices: 29.5 us -> none  [body(): local_x = lax.all_gather(tokens, 'col', axis=0, tiled=True)]
    reduce_scatter x1, waiting for transfers between devices: 3.08 us -> 27.4 us  [body(): lax.psum_scatter(lax.dot_general(full_grad, weight, (((1,), (1,)), ((), (...]
    unnamed x7 -> x23, local copies, waits for them, and re-layouts: 26 us -> 2.8 us
  transfers between devices with their start and end apart: 3 -> 9, of which waited for: 3 -> 9; matrix products, arithmetic and copies ran while one was open for 18% -> 6% of each run, Pallas kernels for 0% -> 0%
where the time goes in v1:
time: 222 us
  waiting for transfers between devices  162 us (73%)
  matrix products  32.3 us (15%)
  between operations  14.2 us (6%)
  other arithmetic  9.37 us (4%)
  local copies, waits for them, and re-layouts  2.81 us (1%)
    psum x1, waiting for transfers between devices, body(): preact = lax.psum(partial_value, 'row') + bias  86 us
    ppermute x7, waiting for transfers between devices, body(): lax.ppermute(ring[-1], 'col', [(dev, (dev + 1) % 8) for dev in range(8)])  48.9 us
    reduce_scatter x1, waiting for transfers between devices, body(): lax.psum_scatter(lax.dot_general(full_grad, weight, (((1,), (1,)), ((), (...  27.4 us
    dot_general x1, matrix products, body(): lax.dot_general(local_x, full_grad, (((0,), (0,)), ((), ())), preferred_e...  10.9 us
    dot_general x1, matrix products, body(): lax.dot_general(full_grad, weight, (((1,), (1,)), ((), ())), preferred_el...  10.7 us
    dot_general x1, matrix products, body(): partial_value = jnp.dot(local_x, weight, preferred_element_type=jnp.float32)  10.7 us
    reduce_sum x1, other arithmetic, body(): grad_bias = jnp.sum(full_grad.astype(jnp.float32), axis=0)  5.49 us
  transfers between devices with their start and end apart: 9, of which 9 were waited for; matrix products, arithmetic and copies ran while one was open for 6% of the time, Pallas kernels for 0%

profile of v1, /device:TPU:0, one launch (start us, length us, event | category | flops | bytes accessed | tf_op | source)
XLA Modules:
  0.0 221.6 jit_solution(11640138434410717313)
XLA Ops:
  7.2 0.0 copy-start.2
  7.2 0.0 all-reduce.2.cloned.1.call-start
  7.2 0.5 collective-permute-start
  7.7 7.6 %collective-permute-done = bf16[32,3072]{1,0:T(8,128)(2,1)S(1)} collective-permute-done((bf16[32,3072]{1,0:T(8,128)(2,1)}, bf16[32,3072]{1,0:T(8,128)(2,1)S(1)}, u32[]{:S(2)}, u32[]{:S(2)}) %collective-permute-start) | collective-permute-done | bytes 196640 | tf_op jit(solution)/shard_map/ppermute | solution.py:21
  15.3 0.0 collective-permute-start.1
  15.3 6.9 %collective-permute-done.1 = bf16[32,3072]{1,0:T(8,128)(2,1)S(1)} collective-permute-done((bf16[32,3072]{1,0:T(8,128)(2,1)S(1)}, bf16[32,3072]{1,0:T(8,128)(2,1)S(1)}, u32[]{:S(2)}, u32[]{:S(2)}) %collective-permute-start.1) | collective-permute-done | bytes 196640 | tf_op jit(solution)/shard_map/ppermute | solution.py:21
  22.2 0.0 collective-permute-start.2
  22.2 6.9 %collective-permute-done.2 = bf16[32,3072]{1,0:T(8,128)(2,1)S(1)} collective-permute-done((bf16[32,3072]{1,0:T(8,128)(2,1)S(1)}, bf16[32,3072]{1,0:T(8,128)(2,1)S(1)}, u32[]{:S(2)}, u32[]{:S(2)}) %collective-permute-start.2) | collective-permute-done | bytes 196640 | tf_op jit(solution)/shard_map/ppermute | solution.py:21
  29.1 0.0 collective-permute-start.3
  29.1 6.9 %collective-permute-done.3 = bf16[32,3072]{1,0:T(8,128)(2,1)S(1)} collective-permute-done((bf16[32,3072]{1,0:T(8,128)(2,1)S(1)}, bf16[32,3072]{1,0:T(8,128)(2,1)S(1)}, u32[]{:S(2)}, u32[]{:S(2)}) %collective-permute-start.3) | collective-permute-done | bytes 196640 | tf_op jit(solution)/shard_map/ppermute | solution.py:21
  36.0 0.0 collective-permute-start.4
  36.0 6.9 %collective-permute-done.4 = bf16[32,3072]{1,0:T(8,128)(2,1)S(1)} collective-permute-done((bf16[32,3072]{1,0:T(8,128)(2,1)S(1)}, bf16[32,3072]{1,0:T(8,128)(2,1)S(1)}, u32[]{:S(2)}, u32[]{:S(2)}) %collective-permute-start.4) | collective-permute-done | bytes 196640 | tf_op jit(solution)/shard_map/ppermute | solution.py:21
  42.9 0.0 collective-permute-start.5
  42.9 6.9 %collective-permute-done.5 = bf16[32,3072]{1,0:T(8,128)(2,1)S(1)} collective-permute-done((bf16[32,3072]{1,0:T(8,128)(2,1)S(1)}, bf16[32,3072]{1,0:T(8,128)(2,1)S(1)}, u32[]{:S(2)}, u32[]{:S(2)}) %collective-permute-start.5) | collective-permute-done | bytes 196640 | tf_op jit(solution)/shard_map/ppermute | solution.py:21
  49.8 0.0 collective-permute-start.6
  49.8 6.9 %collective-permute-done.6 = bf16[32,3072]{1,0:T(8,128)(2,1)S(1)} collective-permute-done((bf16[32,3072]{1,0:T(8,128)(2,1)S(1)}, bf16[32,3072]{1,0:T(8,128)(2,1)S(1)}, u32[]{:S(2)}, u32[]{:S(2)}) %collective-permute-start.6) | collective-permute-done | bytes 196640 | tf_op jit(solution)/shard_map/ppermute | solution.py:21
  56.8 0.9 constant_dynamic-update-slice_fusion.8
  58.0 0.0 copy-done.2
  58.0 0.0 copy-start.1
  58.0 1.6 copy-done.1
  59.6 10.7 %fusion.7 = f32[256,3072]{1,0:T(8,128)} fusion(bf16[3072,3072]{1,0:T(8,128)(2,1)} %param.5, bf16[512,3072]{1,0:T(8,128)(2,1)S(1)} %constant_dynamic-update-slice_fusion, s32[]{:T(128)S(6)} %select_n.17), kind=kOutput, calls=%fused_computation.12 | convolution fusion | flops 4831838208 | bytes 23592964 | tf_op jit(solution)/shard_map/dot_general | solution.py:28
  70.3 0.0 copy-start
  70.3 0.0 copy-start.3
  70.3 0.0 all-reduce.2.cloned.1.call-update
  70.3 0.0 reduce-scatter.2.cloned.1.call-start
  70.4 86.0 %all-reduce.2.cloned.1.call-done = f32[256,3072]{1,0:T(8,128)} async-done(((f32[256,3072]{1,0:T(8,128)}), f32[256,3072]{1,0:T(8,128)}) %all-reduce.2.cloned.1.call-update) | async-done | bytes 3145744 | tf_op jit(solution)/shard_map/psum | solution.py:29
  156.4 0.0 copy-done
  156.4 0.0 copy-done.3
  156.4 5.5 %convert_reduce_fusion = (f32[3072]{0:T(1024)}, bf16[256,3072]{1,0:T(8,128)(2,1)S(1)}, f32[256,3072]{1,0:T(8,128)}, f32[256,3072]{1,0:T(8,128)}) fusion(bf16[256,3072]{1,0:T(8,128)(2,1)S(1)} %copy-done, f32[256,3072]{1,0:T(8,128)} %all-reduce.2.cloned.1.call-done, f32[3072]{0:T(1024)S(1)} %copy-done.3), kind=kLoop, calls=%fused_computation.8 | loop fusion | flops 11006976 | bytes 12607488 | tf_op jit(solution)/shard_map/reduce_sum | solution.py:43
  161.9 10.7 %fusion.13 = f32[256,3072]{1,0:T(8,128)} fusion(bf16[256,3072]{1,0:T(8,128)(2,1)S(1)} %get-tuple-element.5, bf16[3072,3072]{1,0:T(8,128)(2,1)} %param.5), kind=kOutput, calls=%fused_computation.34 | convolution fusion | flops 4831838208 | bytes 23592960 | tf_op jit(solution)/shard_map/dot_general | solution.py:33
  172.6 0.0 reduce-scatter.2.cloned.1.call-update
  172.6 2.2 fusion.9
  174.8 10.9 %convolution_convert_fusion = bf16[3072,3072]{1,0:T(8,128)(2,1)} fusion(bf16[256,3072]{1,0:T(8,128)(2,1)S(1)} %get-tuple-element.5, bf16[512,3072]{1,0:T(8,128)(2,1)} %copy-done.1, s32[]{:T(128)S(6)} %select_n.17), kind=kOutput, calls=%fused_computation | convolution fusion | flops 4841275392 | bytes 22020100 | tf_op jit(solution)/shard_map/dot_general | solution.py:40
  185.7 27.4 %reduce-scatter.2.cloned.1.call-done = f32[32,3072]{1,0:T(8,128)} async-done(((f32[256,3072]{1,0:T(8,128)}), f32[32,3072]{1,0:T(8,128)}) %reduce-scatter.2.cloned.1.call-update) | async-done | bytes 393232 | tf_op jit(solution)/shard_map/reduce_scatter | solution.py:32
  213.1 1.7 convert_element_type.21
  (15 shorter events, 0.2 us)
Async XLA Ops:
  7.2 50.8 %copy-start.2 = (bf16[32,3072]{1,0:T(8,128)(2,1)S(1)}, bf16[32,3072]{1,0:T(8,128)(2,1)}, u32[]{:S(2)}) copy-start(bf16[32,3072]{1,0:T(8,128)(2,1)} %param.4) | copy-start | bytes 589828
  7.2 149.2 %all-reduce.2.cloned.1.call-start = ((), (), s32[]{:S(2)}) async-start(), calls=%async_computation.1 | async-start | bytes 6291456 | tf_op jit(solution)/shard_map/psum | solution.py:29
  7.2 8.1 %collective-permute-start = (bf16[32,3072]{1,0:T(8,128)(2,1)}, bf16[32,3072]{1,0:T(8,128)(2,1)S(1)}, u32[]{:S(2)}, u32[]{:S(2)}) collective-permute-start(bf16[32,3072]{1,0:T(8,128)(2,1)} %param.4), channel_id=1, source_target_pairs={{0,1},{1,2},{2,3},{3,4},{4,5},{5,6},{6,7},{7,0},{8,9},{9,10},{10,1... | collective-permute-start | bytes 589832 | tf_op jit(solution)/shard_map/ppermute | solution.py:21
  15.3 6.9 %collective-permute-start.1 = (bf16[32,3072]{1,0:T(8,128)(2,1)S(1)}, bf16[32,3072]{1,0:T(8,128)(2,1)S(1)}, u32[]{:S(2)}, u32[]{:S(2)}) collective-permute-start(bf16[32,3072]{1,0:T(8,128)(2,1)S(1)} %collective-permute-done), channel_id=1, source_target_pairs={{0,1},{1,2},{2,3},{3,4},{4,5},{5,6},{6,7},{7,0},{8,9},{9,10},{10,1... | collective-permute-start | bytes 589832 | tf_op jit(solution)/shard_map/ppermute | solution.py:21
  22.2 6.9 %collective-permute-start.2 = (bf16[32,3072]{1,0:T(8,128)(2,1)S(1)}, bf16[32,3072]{1,0:T(8,128)(2,1)S(1)}, u32[]{:S(2)}, u32[]{:S(2)}) collective-permute-start(bf16[32,3072]{1,0:T(8,128)(2,1)S(1)} %collective-permute-done.1), channel_id=1, source_target_pairs={{0,1},{1,2},{2,3},{3,4},{4,5},{5,6},{6,7},{7,0},{8,9},{9,10},{10,1... | collective-permute-start | bytes 589832 | tf_op jit(solution)/shard_map/ppermute | solution.py:21
  29.1 6.9 %collective-permute-start.3 = (bf16[32,3072]{1,0:T(8,128)(2,1)S(1)}, bf16[32,3072]{1,0:T(8,128)(2,1)S(1)}, u32[]{:S(2)}, u32[]{:S(2)}) collective-permute-start(bf16[32,3072]{1,0:T(8,128)(2,1)S(1)} %collective-permute-done.2), channel_id=1, source_target_pairs={{0,1},{1,2},{2,3},{3,4},{4,5},{5,6},{6,7},{7,0},{8,9},{9,10},{10,1... | collective-permute-start | bytes 589832 | tf_op jit(solution)/shard_map/ppermute | solution.py:21
  36.0 6.9 %collective-permute-start.4 = (bf16[32,3072]{1,0:T(8,128)(2,1)S(1)}, bf16[32,3072]{1,0:T(8,128)(2,1)S(1)}, u32[]{:S(2)}, u32[]{:S(2)}) collective-permute-start(bf16[32,3072]{1,0:T(8,128)(2,1)S(1)} %collective-permute-done.3), channel_id=1, source_target_pairs={{0,1},{1,2},{2,3},{3,4},{4,5},{5,6},{6,7},{7,0},{8,9},{9,10},{10,1... | collective-permute-start | bytes 589832 | tf_op jit(solution)/shard_map/ppermute | solution.py:21
  42.9 6.9 %collective-permute-start.5 = (bf16[32,3072]{1,0:T(8,128)(2,1)S(1)}, bf16[32,3072]{1,0:T(8,128)(2,1)S(1)}, u32[]{:S(2)}, u32[]{:S(2)}) collective-permute-start(bf16[32,3072]{1,0:T(8,128)(2,1)S(1)} %collective-permute-done.4), channel_id=1, source_target_pairs={{0,1},{1,2},{2,3},{3,4},{4,5},{5,6},{6,7},{7,0},{8,9},{9,10},{10,1... | collective-permute-start | bytes 589832 | tf_op jit(solution)/shard_map/ppermute | solution.py:21
  49.8 6.9 %collective-permute-start.6 = (bf16[32,3072]{1,0:T(8,128)(2,1)S(1)}, bf16[32,3072]{1,0:T(8,128)(2,1)S(1)}, u32[]{:S(2)}, u32[]{:S(2)}) collective-permute-start(bf16[32,3072]{1,0:T(8,128)(2,1)S(1)} %collective-permute-done.5), channel_id=1, source_target_pairs={{0,1},{1,2},{2,3},{3,4},{4,5},{5,6},{6,7},{7,0},{8,9},{9,10},{10,1... | collective-permute-start | bytes 589832 | tf_op jit(solution)/shard_map/ppermute | solution.py:21
  58.0 1.6 copy-start.1
  70.3 86.1 %copy-start = (bf16[256,3072]{1,0:T(8,128)(2,1)S(1)}, bf16[256,3072]{1,0:T(8,128)(2,1)}, u32[]{:S(2)}) copy-start(bf16[256,3072]{1,0:T(8,128)(2,1)} %param.7) | copy-start | bytes 4718596
  70.3 86.1 %copy-start.3 = (f32[3072]{0:T(1024)S(1)}, f32[3072]{0:T(1024)}, u32[]{:S(2)}) copy-start(f32[3072]{0:T(1024)} %param.6) | copy-start | bytes 36868
  70.3 142.8 %reduce-scatter.2.cloned.1.call-start = ((), (), s32[]{:S(2)}) async-start(), calls=%async_computation.2 | async-start | bytes 3538944 | tf_op jit(solution)/shard_map/reduce_scatter | solution.py:32
Sparse Core Ops, SparseCore 0:
  70.4 85.8 all-reduce.1
  172.7 40.3 reduce-scatter.1
